TPU v7x, 32 devices: a whole 2x2x4 slice. The times are simulated.
32 devices in a mesh: fsdp: 4 (over y, x), seq: 8 (over z, core).
Axes of the slice: x: 2, y: 2, z: 4, core: 2. Of those that a mesh axis runs over, the one named last changes fastest.
Arguments:
- events: bfloat16 [4, 1024, 2048], P('fsdp', 'seq'), may hold values from -6 to 6
- type_ids: int32 [4, 1024], P('fsdp', 'seq'), may hold values from 0 to 255
- type_table: bfloat16 [256, 2048], P('fsdp'), may hold values from -6 to 6
- norm_gain: float32 [2048], replicated, may hold values from 0.25 to 1.75
- kernel: bfloat16 [2048, 1152], P('fsdp'), may hold values from -0.1875 to 0.1875
- upstream: bfloat16 [4, 1024, 2048], P('fsdp', 'seq'), may hold values from -6 to 6
Outputs:
- input_grad: bfloat16 [4, 1024, 2048], P('fsdp', 'seq')
- table_grad: float32 [256, 2048], P(('fsdp', 'seq'))
- gain_grad: float32 [2048], P(('fsdp', 'seq'))
- kernel_grad: float32 [2048, 1152], P('seq')
All inputs are finite; a program needn't handle non-finite values.
Results may differ from a plain program's by a relative error of at most 0.0053.
Values may be sent and summed in bfloat16 or wider, within the bound.
No kernel may reach another device: no remote copies, remote signals or barrier semaphores. Data moves between devices by JAX's collectives and lax.ppermute only.
A program may use at most 128 MiB of HBM per device.

v0:
```python
import jax
import jax.numpy as jnp
from jax import lax
from jax.sharding import PartitionSpec as P

GROUPS = 16
KERNEL = 9


def with_halo(cells, axis, dim, width):
    count = lax.axis_size(axis)
    ends = count - 1
    head = lax.slice_in_dim(cells, 0, width, axis=dim)
    tail = lax.slice_in_dim(cells, cells.shape[dim] - width, cells.shape[dim], axis=dim)
    return jnp.concatenate(
        [
            lax.ppermute(tail, axis, [(i, (i + 1) % count) for i in range(ends)]),
            cells,
            lax.ppermute(head, axis, [((i + 1) % count, i) for i in range(ends)]),
        ],
        axis=dim,
    )


def from_partner(value, axis, apart):
    mask = 2**apart
    pairs = [(source, source ^ mask) for source in range(lax.axis_size(axis))]
    return lax.ppermute(value, axis, pairs)


def gather_rows(block, axis):
    count = lax.axis_size(axis)
    return lax.all_to_all(
        jnp.tile(block, (count,) + (1,) * (block.ndim - 1)), axis, 0, 0, tiled=True
    )


def conv_forward(padded, weights, length):
    chans = padded.shape[-1]
    total = None
    for k in range(KERNEL):
        term = jnp.einsum(
            "gtc,goc->gto",
            padded[:, k : k + length],
            weights[:, :, k * chans : (k + 1) * chans],
            preferred_element_type=jnp.float32,
        )
        total = term if total is None else total + term
    return total


def conv_backward(dpad, weights, length):
    chans = weights.shape[-1] // KERNEL
    half = KERNEL // 2
    total = None
    for k in range(KERNEL):
        term = jnp.einsum(
            "gto,goc->gtc",
            dpad[:, 2 * half - k : 2 * half - k + length],
            weights[:, :, k * chans : (k + 1) * chans],
            preferred_element_type=jnp.float32,
        )
        total = term if total is None else total + term
    return total


def spread_groups(normed, dflat, chans):
    normed_slice = lax.all_to_all(normed, "seq", 1, 0, tiled=True)
    dconv_slice = lax.all_to_all(dflat, "seq", 1, 0, tiled=True)
    whole, slice_width = normed_slice.shape
    spread = chans // slice_width
    position = lax.axis_index("seq")
    group_rows = normed_slice
    for bit in range(spread.bit_length() - 1):
        partner = from_partner(group_rows, "seq", bit)
        lower = position >> bit & 1 == 0
        group_rows = jnp.where(
            lower,
            jnp.concatenate([group_rows, partner], axis=1),
            jnp.concatenate([partner, group_rows], axis=1),
        )
    return (group_rows.reshape(1, whole, chans), dconv_slice.reshape(1, whole, slice_width))


def sum_rows(block, axis):
    count = lax.axis_size(axis)
    parts = block.reshape(count, block.shape[0] // count, *block.shape[1:])
    return lax.all_to_all(parts, axis, 0, 0, tiled=True).sum(axis=0)


def psum_rows(block, axis):
    return gather_rows(sum_rows(block, axis), axis)


def table_and_gain(input_grad, ids, gain_term, types, scale):
    every = ("fsdp", "seq")
    count = lax.axis_size("fsdp") * lax.axis_size("seq")
    length, width = input_grad.shape
    narrow = width // count
    id_rows = -(-length // narrow)
    ids_wide = (
        jnp.zeros((id_rows * narrow,), jnp.bfloat16).at[:length].set(ids.astype(jnp.bfloat16))
    )
    send = jnp.concatenate(
        [
            input_grad.reshape(length, count, narrow).transpose(1, 0, 2),
            jnp.broadcast_to(ids_wide.reshape(1, id_rows, narrow), (count, id_rows, narrow)),
        ],
        axis=1,
    )
    got = lax.all_to_all(send, every, 0, 0, tiled=True)
    rows_all = got[:, :length].reshape(count * length, narrow)
    ids_all = (
        got[:, length:].reshape(count, id_rows * narrow)[:, :length].reshape(-1).astype(jnp.int32)
    )
    onehot = (ids_all[:, None] == jnp.arange(types, dtype=jnp.int32)[None, :]).astype(jnp.bfloat16)
    columns = lax.dot_general(
        onehot, rows_all, (((0,), (0,)), ((), ())), preferred_element_type=jnp.float32
    )
    columns = columns * scale
    per = types // count
    back = jnp.concatenate(
        [columns.reshape(count, per, narrow), gain_term.reshape(count, 1, narrow)], axis=1
    )
    back = lax.all_to_all(back, every, 0, 0, tiled=True)
    table_grad = back[:, :per].transpose(1, 0, 2).reshape(per, width)
    gain_grad = back[:, per].sum(axis=0)
    return (table_grad, gain_grad)


def body(events, type_ids, type_table, norm_gain, kernel, upstream):
    length = events.shape[1]
    width = events.shape[2]
    chans = width // GROUPS
    half = KERNEL // 2
    fsdp = lax.axis_size("fsdp")
    seq_count = lax.axis_size("seq")
    total = length * seq_count * fsdp
    scale = 1.0 / jnp.sqrt(jnp.float32(total))
    table = gather_rows(type_table, "fsdp")
    types = table.shape[0]
    onehot = (type_ids[0][:, None] == jnp.arange(types, dtype=jnp.int32)[None, :]).astype(
        jnp.bfloat16
    )
    mixed = events[0].astype(jnp.float32) + jnp.dot(
        onehot, table, preferred_element_type=jnp.float32
    )
    inv = lax.rsqrt(jnp.mean(mixed * mixed, axis=-1, keepdims=True) + 1e-06)
    normed = (mixed * inv * norm_gain).astype(jnp.bfloat16)
    normed_g = normed.reshape(length, GROUPS, chans).transpose(1, 0, 2)
    padded = with_halo(normed_g, "seq", 1, half)
    weights = lax.all_gather(kernel, "fsdp", axis=0, tiled=True).reshape(
        GROUPS, chans, KERNEL * chans
    )
    conv = conv_forward(padded, weights, length)
    up_float = upstream[0].astype(jnp.float32)
    up_g = up_float.reshape(length, GROUPS, chans).transpose(1, 0, 2)
    sig = jax.nn.sigmoid(conv)
    dconv = (up_g * sig * (1.0 + conv * (1.0 - sig))).astype(jnp.bfloat16)
    dpad = with_halo(dconv, "seq", 1, half)
    dnormed = conv_backward(dpad, weights, length)
    if seq_count <= GROUPS:
        group_in = lax.all_to_all(normed_g, "seq", 0, 1, tiled=True)
        group_out = lax.all_to_all(dconv, "seq", 0, 1, tiled=True)
    else:
        group_in, group_out = spread_groups(
            normed, dconv.transpose(1, 0, 2).reshape(length, width), chans
        )
    local_groups = group_in.shape[0]
    whole = group_in.shape[1]
    group_pad = jnp.pad(group_in, ((0, 0), (half, half), (0, 0)))
    kterms = [
        jnp.einsum(
            "gto,gtc->goc",
            group_out,
            group_pad[:, k : k + whole],
            preferred_element_type=jnp.float32,
        )
        for k in range(KERNEL)
    ]
    kernel_part = jnp.concatenate(kterms, axis=-1).reshape(-1, KERNEL * chans) * scale
    dnormed = dnormed.transpose(1, 0, 2).reshape(length, width)
    gain_term = jnp.sum(dnormed * mixed * inv, axis=0) * scale
    scaled = norm_gain * dnormed
    dmixed = inv * scaled - mixed * inv * inv * inv * jnp.mean(
        scaled * mixed, axis=-1, keepdims=True
    )
    input_grad = (up_float + dmixed).astype(jnp.bfloat16)
    kernel_grad = lax.psum(kernel_part, "fsdp")
    table_grad, gain_grad = table_and_gain(input_grad, type_ids[0], gain_term, types, scale)
    return (input_grad[None], table_grad, gain_grad, kernel_grad)


def solution(mesh):
    return jax.shard_map(
        body,
        mesh=mesh,
        in_specs=(
            P("fsdp", "seq", None),
            P("fsdp", "seq"),
            P("fsdp", None),
            P(),
            P("fsdp", None),
            P("fsdp", "seq", None),
        ),
        out_specs=(
            P("fsdp", "seq", None),
            P(("fsdp", "seq"), None),
            P(("fsdp", "seq")),
            P("seq", None),
        ),
        check_vma=False,
    )
```

profile of v0, /device:TPU:0, one launch (start us, length us, event | category | flops | bytes accessed | tf_op | source)
XLA Modules:
  0.0 202.8 jit_solution(586247132597513163)
XLA Ops:
  7.2 0.7 all-gather.2.cloned.1.call-update
  7.9 1.1 tile.2
  9.1 24.3 %all_to_all.55 = bf16[4,64,2048]{2,1,0:T(8,128)(2,1)S(1)} all-to-all(bf16[4,64,2048]{2,1,0:T(8,128)(2,1)S(1)} %tile.2), channel_id=1, replica_groups=mesh['fsdp'=4,'seq'=8] {'fsdp'}, dimensions={0} | all-to-all | bytes 2097152 | tf_op jit(solution)/shard_map/all_to_all | solution.py:33
  33.4 0.4 multiply_reduce_fusion.2
  33.8 1.0 bitcast_bitcast_fusion
  34.8 5.2 %all-to-all-start.4 = ((bf16[16,128,128]{2,1,0:T(8,128)(2,1)}), bf16[16,128,128]{2,1,0:T(8,128)(2,1)S(1)}, u32[]{:S(2)}, u32[]{:S(2)}) async-start(bf16[16,128,128]{2,1,0:T(8,128)(2,1)} %bitcast_bitcast_fusion), calls=%async_computation.4 | async-start | bytes 1048576 | tf_op jit(solution)/shard_map/all_to_all | solution.py:163
  40.1 0.2 copy.126
  40.5 0.8 fusion.148
  41.3 2.4 %collective-permute-start = (bf16[16,4,128]{2,1,0:T(4,128)(2,1)S(1)}, bf16[16,4,128]{2,1,0:T(4,128)(2,1)S(1)}, u32[]{:S(2)}, u32[]{:S(2)}) collective-permute-start(bf16[16,4,128]{2,1,0:T(4,128)(2,1)S(1)} %get-tuple-element.28), channel_id=1, source_target_pairs={{0,1},{1,2},{2,3},{3,4},{4,5},{5,6},{6,7},{8,9},{9,10},{10,11},{11... | collective-permute-start | bytes 49160 | tf_op jit(solution)/shard_map/ppermute | solution.py:17
  43.7 1.3 collective-permute-start.1
  45.0 10.3 %all-to-all-done.4 = bf16[16,128,128]{2,1,0:T(8,128)(2,1)S(1)} async-done(((bf16[16,128,128]{2,1,0:T(8,128)(2,1)}), bf16[16,128,128]{2,1,0:T(8,128)(2,1)S(1)}, u32[]{:S(2)}, u32[]{:S(2)}) %all-to-all-start.4) | async-done | bytes 524320 | tf_op jit(solution)/shard_map/all_to_all | solution.py:163
  55.3 0.3 copy.111
  55.6 1.0 all_to_all.49
  56.7 17.2 %all-gather.2.cloned.1.call-done = bf16[2048,1152]{1,0:T(8,128)(2,1)} async-done(((bf16[512,1152]{1,0:T(8,128)(2,1)}), bf16[2048,1152]{1,0:T(8,128)(2,1)}) %all-gather.2.cloned.1.call-update) | async-done | bytes 4718608 | tf_op jit(solution)/shard_map/all_gather | solution.py:152
  73.8 1.7 fusion.92
  75.6 1.7 fusion.44
  77.2 1.5 fusion.49
  78.8 1.5 fusion.69
  80.3 1.5 fusion.41
  81.8 1.5 fusion.36
  83.4 1.5 fusion.64
  84.9 1.6 fusion.13
  86.5 2.8 %fusion.18 = bf16[16,128,128]{2,1,0:T(8,128)(2,1)} fusion(f32[128,16,128]{2,1,0:T(8,128)S(1)} %bitcast.108, f32[16,128,128]{2,1,0:T(8,128)S(1)} %fusion.64, f32[16,128,128]{2,1,0:T(8,128)S(1)} %fusion.36, f32[16,128,128]{2,1,0:T(8,128)S(1)} %fusion.41, f32[16,128,128]{2,1,0:T(8,128)S(1)} %fusion.13, bf16[16,4,128]{2,1,0:T(4,128)(2,1)S(1)} %collective-permute-done.1, ...), kind=kOutput, calls=%fused_computation.37 | convolution fusion | flops 71565312 | bytes 6832128 | tf_op jit(solution)/shard_map/gtc,goc->gto/dot_general | solution.py:42
  89.3 4.6 %all-to-all-start.3 = ((bf16[16,128,128]{2,1,0:T(8,128)(2,1)}), bf16[16,128,128]{2,1,0:T(8,128)(2,1)}, u32[]{:S(2)}, u32[]{:S(2)}) async-start(bf16[16,128,128]{2,1,0:T(8,128)(2,1)} %fusion.18), calls=%async_computation.3 | async-start | bytes 1048576 | tf_op jit(solution)/shard_map/all_to_all | solution.py:164
  93.9 0.8 fusion.147
  94.8 1.3 collective-permute-start.2
  96.1 1.7 fusion.90
  97.8 3.0 %collective-permute-start.3 = (bf16[16,4,128]{2,1,0:T(4,128)(2,1)S(1)}, bf16[16,4,128]{2,1,0:T(4,128)(2,1)S(1)}, u32[]{:S(2)}, u32[]{:S(2)}) collective-permute-start(bf16[16,4,128]{2,1,0:T(4,128)(2,1)S(1)} %get-tuple-element.27), channel_id=1, source_target_pairs={{0,1},{1,2},{2,3},{3,4},{4,5},{5,6},{6,7},{8,9},{9,10},{10,11},{11... | collective-permute-start | bytes 49160 | tf_op jit(solution)/shard_map/ppermute | solution.py:17
  100.8 1.7 fusion.33
  102.5 1.7 fusion.28
  104.3 1.7 fusion.59
  106.0 1.7 fusion.25
  107.7 1.7 fusion.20
  109.4 1.7 fusion.54
  111.1 1.7 fusion.7
  112.9 1.8 fusion.4
  114.6 0.3 copy.122
  115.0 0.3 multiply_reduce_fusion
  115.3 1.4 fusion.16
  116.7 0.3 copy.102
  117.1 1.3 pad_maximum_fusion
  118.4 9.9 %all-to-all-start.1 = ((bf16[32,130,64]{1,2,0:T(8,128)(2,1)}), bf16[32,130,64]{1,2,0:T(8,128)(2,1)S(1)}, u32[]{:S(2)}, u32[]{:S(2)}) async-start(bf16[32,130,64]{1,2,0:T(8,128)(2,1)} %pad_maximum_fusion), calls=%async_computation.1 | async-start | bytes 2097152 | tf_op jit(solution)/shard_map/all_to_all | solution.py:111
  128.3 0.2 all-reduce.3.cloned.1.call-start
  128.6 1.1 copy.110
  129.6 0.4 convolution_dynamic-update-slice_fusion.8
  130.0 0.4 convolution_dynamic-update-slice_fusion.7
  130.4 0.4 convolution_dynamic-update-slice_fusion.6
  130.7 0.4 convolution_dynamic-update-slice_fusion.5
  131.1 0.3 convolution_dynamic-update-slice_fusion.4
  131.4 0.4 convolution_dynamic-update-slice_fusion.3
  131.8 0.4 convolution_dynamic-update-slice_fusion.2
  132.1 0.4 convolution_dynamic-update-slice_fusion.1
  132.5 0.4 convolution_dynamic-update-slice_fusion
  133.0 1.4 copy.112
  134.5 21.5 %all-to-all-done.1 = bf16[32,130,64]{1,2,0:T(8,128)(2,1)S(1)} async-done(((bf16[32,130,64]{1,2,0:T(8,128)(2,1)}), bf16[32,130,64]{1,2,0:T(8,128)(2,1)S(1)}, u32[]{:S(2)}, u32[]{:S(2)}) %all-to-all-start.1) | async-done | bytes 532512 | tf_op jit(solution)/shard_map/all_to_all | solution.py:111
  156.0 0.3 copy.123
  156.4 0.9 fusion.14
  157.6 9.6 %all_to_all.56 = f32[32,1,576]{2,1,0:T(1,128)S(1)} all-to-all(f32[32,1,576]{2,1,0:T(1,128)S(1)} %reshape.125), channel_id=1, replica_groups=mesh['fsdp'=4,'seq'=8] {'fsdp','seq'}, dimensions={0} | all-to-all | bytes 147456 | tf_op jit(solution)/shard_map/all_to_all | solution.py:125
  167.2 0.5 broadcast.63
  167.7 0.8 reduce.7
  168.7 0.7 reshape.113
  169.4 0.6 slice_reduce_fusion
  170.0 23.7 %all-reduce.3.cloned.1.call-done = f32[256,1152]{1,0:T(8,128)} async-done(((f32[256,1152]{1,0:T(8,128)}), f32[256,1152]{1,0:T(8,128)}) %all-reduce.3.cloned.1.call-update) | async-done | bytes 1179664 | tf_op jit(solution)/shard_map/psum | solution.py:189
  193.6 2.4 %copy.143 = f32[256,1152]{1,0:T(8,128)} copy(f32[256,1152]{1,0:T(8,128)} %all-reduce.3.cloned.1.call-done) | data formatting | bytes 2359296
  (41 shorter events, 1.3 us)
Async XLA Ops:
  7.2 26.2 %copy-start.6 = (s32[1,128]{1,0:T(1,128)S(1)}, s32[1,128]{1,0:T(1,128)}, u32[]{:S(2)}) copy-start(s32[1,128]{1,0:T(1,128)} %param.11) | copy-start | bytes 1540
  7.2 26.2 %copy-start.4 = (bf16[1,128,2048]{2,1,0:T(8,128)(2,1)S(1)}, bf16[1,128,2048]{2,1,0:T(8,128)(2,1)}, u32[]{:S(2)}) copy-start(bf16[1,128,2048]{2,1,0:T(8,128)(2,1)} %param.10) | copy-start | bytes 1572868
  7.2 26.6 %copy-start.5 = (f32[2048]{0:T(1024)S(1)}, f32[2048]{0:T(1024)}, u32[]{:S(2)}) copy-start(f32[2048]{0:T(1024)} %param.13) | copy-start | bytes 24580
  7.2 66.6 %all-gather.2.cloned.1.call-start = ((), (), s32[]{:S(2)}) async-start(), calls=%async_computation.5 | async-start | bytes 5898240 | tf_op jit(solution)/shard_map/all_gather | solution.py:152
  7.9 32.0 %copy-start.1 = (bf16[1,128,2048]{2,1,0:T(8,128)(2,1)S(1)}, bf16[1,128,2048]{2,1,0:T(8,128)(2,1)}, u32[]{:S(2)}) copy-start(bf16[1,128,2048]{2,1,0:T(8,128)(2,1)} %param.15) | copy-start | bytes 1572868
  34.8 20.5 %all-to-all-start.4 = ((bf16[16,128,128]{2,1,0:T(8,128)(2,1)}), bf16[16,128,128]{2,1,0:T(8,128)(2,1)S(1)}, u32[]{:S(2)}, u32[]{:S(2)}) async-start(bf16[16,128,128]{2,1,0:T(8,128)(2,1)} %bitcast_bitcast_fusion), calls=%async_computation.4 | async-start | bytes 1048576 | tf_op jit(solution)/shard_map/all_to_all | solution.py:163
  41.3 34.3 %collective-permute-start = (bf16[16,4,128]{2,1,0:T(4,128)(2,1)S(1)}, bf16[16,4,128]{2,1,0:T(4,128)(2,1)S(1)}, u32[]{:S(2)}, u32[]{:S(2)}) collective-permute-start(bf16[16,4,128]{2,1,0:T(4,128)(2,1)S(1)} %get-tuple-element.28), channel_id=1, source_target_pairs={{0,1},{1,2},{2,3},{3,4},{4,5},{5,6},{6,7},{8,9},{9,10},{10,11},{11... | collective-permute-start | bytes 49160 | tf_op jit(solution)/shard_map/ppermute | solution.py:17
  43.7 36.6 %collective-permute-start.1 = (bf16[16,4,128]{2,1,0:T(4,128)(2,1)S(1)}, bf16[16,4,128]{2,1,0:T(4,128)(2,1)S(1)}, u32[]{:S(2)}, u32[]{:S(2)}) collective-permute-start(bf16[16,4,128]{2,1,0:T(4,128)(2,1)S(1)} %get-tuple-element.29), channel_id=1, source_target_pairs={{1,0},{2,1},{3,2},{4,3},{5,4},{6,5},{7,6},{9,8},{10,9},{11,10},{12... | collective-permute-start | bytes 49160 | tf_op jit(solution)/shard_map/ppermute | solution.py:19
  73.8 3.4 %copy-start = (bf16[2048,1152]{1,0:T(8,128)(2,1)S(1)}, bf16[2048,1152]{1,0:T(8,128)(2,1)}, u32[]{:S(2)}) copy-start(bf16[2048,1152]{1,0:T(8,128)(2,1)} %all-gather.2.cloned.1.call-done) | copy-start | bytes 14155780
  89.3 29.1 %all-to-all-start.3 = ((bf16[16,128,128]{2,1,0:T(8,128)(2,1)}), bf16[16,128,128]{2,1,0:T(8,128)(2,1)}, u32[]{:S(2)}, u32[]{:S(2)}) async-start(bf16[16,128,128]{2,1,0:T(8,128)(2,1)} %fusion.18), calls=%async_computation.3 | async-start | bytes 1048576 | tf_op jit(solution)/shard_map/all_to_all | solution.py:164
  94.8 6.1 %collective-permute-start.2 = (bf16[16,4,128]{2,1,0:T(4,128)(2,1)S(1)}, bf16[16,4,128]{2,1,0:T(4,128)(2,1)S(1)}, u32[]{:S(2)}, u32[]{:S(2)}) collective-permute-start(bf16[16,4,128]{2,1,0:T(4,128)(2,1)S(1)} %get-tuple-element.26), channel_id=1, source_target_pairs={{1,0},{2,1},{3,2},{4,3},{5,4},{6,5},{7,6},{9,8},{10,9},{11,10},{12... | collective-permute-start | bytes 49160 | tf_op jit(solution)/shard_map/ppermute | solution.py:19
  97.8 8.2 %collective-permute-start.3 = (bf16[16,4,128]{2,1,0:T(4,128)(2,1)S(1)}, bf16[16,4,128]{2,1,0:T(4,128)(2,1)S(1)}, u32[]{:S(2)}, u32[]{:S(2)}) collective-permute-start(bf16[16,4,128]{2,1,0:T(4,128)(2,1)S(1)} %get-tuple-element.27), channel_id=1, source_target_pairs={{0,1},{1,2},{2,3},{3,4},{4,5},{5,6},{6,7},{8,9},{9,10},{10,11},{11... | collective-permute-start | bytes 49160 | tf_op jit(solution)/shard_map/ppermute | solution.py:17
  116.7 13.7 %copy-start.3 = (bf16[128,2048]{1,0:T(8,128)(2,1)}, bf16[128,2048]{1,0:T(8,128)(2,1)S(1)}, u32[]{:S(2)}) copy-start(bf16[128,2048]{1,0:T(8,128)(2,1)S(1)} %fusion.16) | copy-start | bytes 1572868
  116.7 12.9 %copy-start.2 = (bf16[2,1024,128]{1,2,0:T(8,128)(2,1)S(1)}, bf16[2,1024,128]{1,2,0:T(8,128)(2,1)}, u32[]{:S(2)}) copy-start(bf16[2,1024,128]{1,2,0:T(8,128)(2,1)} %all_to_all.49) | copy-start | bytes 1572868
  118.4 37.5 %all-to-all-start.1 = ((bf16[32,130,64]{1,2,0:T(8,128)(2,1)}), bf16[32,130,64]{1,2,0:T(8,128)(2,1)S(1)}, u32[]{:S(2)}, u32[]{:S(2)}) async-start(bf16[32,130,64]{1,2,0:T(8,128)(2,1)} %pad_maximum_fusion), calls=%async_computation.1 | async-start | bytes 2097152 | tf_op jit(solution)/shard_map/all_to_all | solution.py:111
  128.3 65.3 %all-reduce.3.cloned.1.call-start = ((), (), s32[]{:S(2)}) async-start(), calls=%async_computation.6 | async-start | bytes 2359296 | tf_op jit(solution)/shard_map/psum | solution.py:189
Sparse Core Ops, SparseCore 0:
  9.9 63.9 all-gather.1
  134.5 59.0 all-reduce.2
where the time goes:
time: 204 us; the launch traced here: 203 us
  waiting for transfers between devices  73.3 us (36%)
  matrix products  35.4 us (17%)
  blocking collectives  33.9 us (17%)
  starting transfers between devices  28 us (14%)
  between operations  14.5 us (7%)
  local copies, waits for them, and re-layouts  12.2 us (6%)
  other arithmetic  5.63 us (3%)
    all_to_all x1, blocking collectives, gather_rows(): lax.all_to_all(jnp.tile(block, (count,) + (1,) * (block.ndim - 1)), axis,...  24.3 us
    psum x1, waiting for transfers between devices, body(): kernel_grad = lax.psum(kernel_part, 'fsdp')  23.7 us
    all_to_all x1, waiting for transfers between devices, table_and_gain(): got = lax.all_to_all(send, every, 0, 0, tiled=True)  21.5 us
    all_gather x1, waiting for transfers between devices, body(): lax.all_gather(kernel, 'fsdp', axis=0, tiled=True)  17.2 us
    dot_general x9, matrix products, conv_backward(): jnp.einsum('gto,goc->gtc', dpad[:, 2 * half - k:2 * half - k + length], w...  15.5 us
    dot_general x9, matrix products, conv_forward(): jnp.einsum('gtc,goc->gto', padded[:, k:k + length], weights[:, :, k * cha...  15.4 us
    all_to_all x1, waiting for transfers between devices, body(): group_in = lax.all_to_all(normed_g, 'seq', 0, 1, tiled=True)  10.3 us
    all_to_all x1, starting transfers between devices, table_and_gain(): got = lax.all_to_all(send, every, 0, 0, tiled=True)  9.92 us
  transfers between devices with their start and end apart: 9, of which 4 were waited for; matrix products, arithmetic and copies ran while one was open for 20% of the time, Pallas kernels for 0%

commit v1 on v0

--- a/solution.py
+++ b/solution.py
@@ -186,7 +186,8 @@
         scaled * mixed, axis=-1, keepdims=True
     )
     input_grad = (up_float + dmixed).astype(jnp.bfloat16)
-    kernel_grad = lax.psum(kernel_part, "fsdp")
+    blocks = lax.all_gather(kernel_part, "fsdp", axis=0, tiled=False)
+    kernel_grad = blocks.sum(axis=0)
     table_grad, gain_grad = table_and_gain(input_grad, type_ids[0], gain_term, types, scale)
     return (input_grad[None], table_grad, gain_grad, kernel_grad)
 

time: 204 us -> 196 us (0.961)
  blocking collectives: 33.9 us -> 9.7 us
  waiting for transfers between devices: 73.3 us -> 90.4 us
  other arithmetic: 5.63 us -> 9.37 us
  local copies, waits for them, and re-layouts: 12.2 us -> 8.9 us
    all_to_all x1 -> x0, blocking collectives: 24.3 us -> none  [gather_rows(): lax.all_to_all(jnp.tile(block, (count,) + (1,) * (block.ndim - 1)), axis,...]
    psum x1 -> x0, waiting for transfers between devices: 23.7 us -> none  [body(): kernel_grad = lax.psum(kernel_part, 'fsdp')]
    all_to_all x0 -> x1, waiting for transfers between devices: none -> 20.3 us  [gather_rows(): lax.all_to_all(jnp.tile(block, (count,) + (1,) * (block.ndim - 1)), axis,...]
    all_to_all x1, waiting for transfers between devices: 0.01 us -> 14.8 us  [body(): group_out = lax.all_to_all(dconv, 'seq', 0, 1, tiled=True)]
    all_to_all x1, waiting for transfers between devices: 10.3 us -> 0.01 us  [body(): group_in = lax.all_to_all(normed_g, 'seq', 0, 1, tiled=True)]
    all_gather x1, waiting for transfers between devices: 17.2 us -> 27.1 us  [body(): lax.all_gather(kernel, 'fsdp', axis=0, tiled=True)]
    all_to_all x1, starting transfers between devices: 9.92 us -> 2.82 us  [table_and_gain(): got = lax.all_to_all(send, every, 0, 0, tiled=True)]
    all_to_all x1, waiting for transfers between devices: 21.5 us -> 27.5 us  [table_and_gain(): got = lax.all_to_all(send, every, 0, 0, tiled=True)]
  transfers between devices with their start and end apart: 9 -> 10, of which waited for: 4 -> 4; matrix products, arithmetic and copies ran while one was open for 20% -> 23% of each run, Pallas kernels for 0% -> 0%
where the time goes in v1:
time: 196 us; the launch traced here: 195 us
  waiting for transfers between devices  90.4 us (46%)
  matrix products  35.6 us (18%)
  starting transfers between devices  26.6 us (14%)
  between operations  14.5 us (7%)
  blocking collectives  9.7 us (5%)
  other arithmetic  9.37 us (5%)
  local copies, waits for them, and re-layouts  8.9 us (5%)
    all_to_all x1, waiting for transfers between devices, table_and_gain(): got = lax.all_to_all(send, every, 0, 0, tiled=True)  27.5 us
    all_gather x1, waiting for transfers between devices, body(): lax.all_gather(kernel, 'fsdp', axis=0, tiled=True)  27.1 us
    all_to_all x1, waiting for transfers between devices, gather_rows(): lax.all_to_all(jnp.tile(block, (count,) + (1,) * (block.ndim - 1)), axis,...  20.3 us
    dot_general x9, matrix products, conv_forward(): jnp.einsum('gtc,goc->gto', padded[:, k:k + length], weights[:, :, k * cha...  15.4 us
    all_to_all x1, waiting for transfers between devices, body(): group_out = lax.all_to_all(dconv, 'seq', 0, 1, tiled=True)  14.8 us
    dot_general x9, matrix products, conv_backward(): jnp.einsum('gto,goc->gtc', dpad[:, 2 * half - k:2 * half - k + length], w...  14.7 us
    all_to_all x1, blocking collectives, table_and_gain(): back = lax.all_to_all(back, every, 0, 0, tiled=True)  9.7 us
    ppermute x2, starting transfers between devices, with_halo(): lax.ppermute(tail, axis, [(i, (i + 1) % count) for i in range(ends)])  5.72 us
  transfers between devices with their start and end apart: 10, of which 4 were waited for; matrix products, arithmetic and copies ran while one was open for 23% of the time, Pallas kernels for 0%

profile of v1, /device:TPU:0, one launch (start us, length us, event | category | flops | bytes accessed | tf_op | source)
XLA Modules:
  0.0 195.0 jit_solution(3387529353202595104)
XLA Ops:
  7.2 0.7 all-gather.3.cloned.1.call-update
  7.9 2.0 %tile.2 = bf16[4,64,2048]{2,1,0:T(8,128)(2,1)} broadcast(bf16[64,2048]{1,0:T(8,128)(2,1)} %param.12), dimensions={1,2} | broadcast | bytes 1310720 | tf_op jit(solution)/shard_map/tile | solution.py:34
  10.0 5.3 %all-to-all-start = ((bf16[4,64,2048]{2,1,0:T(8,128)(2,1)}), bf16[4,64,2048]{2,1,0:T(8,128)(2,1)S(1)}, u32[]{:S(2)}, u32[]{:S(2)}) async-start(bf16[4,64,2048]{2,1,0:T(8,128)(2,1)} %tile.2), calls=%async_computation | async-start | bytes 2097152 | tf_op jit(solution)/shard_map/all_to_all | solution.py:33
  15.4 0.2 copy.148
  15.6 20.3 %all-to-all-done = bf16[4,64,2048]{2,1,0:T(8,128)(2,1)S(1)} async-done(((bf16[4,64,2048]{2,1,0:T(8,128)(2,1)}), bf16[4,64,2048]{2,1,0:T(8,128)(2,1)S(1)}, u32[]{:S(2)}, u32[]{:S(2)}) %all-to-all-start) | async-done | bytes 1048608 | tf_op jit(solution)/shard_map/all_to_all | solution.py:33
  35.9 1.5 multiply_reduce_fusion.2
  37.4 1.0 bitcast_bitcast_fusion
  38.4 5.2 %all-to-all-start.4 = ((bf16[16,128,128]{2,1,0:T(8,128)(2,1)}), bf16[16,128,128]{2,1,0:T(8,128)(2,1)S(1)}, u32[]{:S(2)}, u32[]{:S(2)}) async-start(bf16[16,128,128]{2,1,0:T(8,128)(2,1)} %bitcast_bitcast_fusion), calls=%async_computation.4 | async-start | bytes 1048576 | tf_op jit(solution)/shard_map/all_to_all | solution.py:163
  43.6 0.8 fusion.148
  44.4 2.4 %collective-permute-start = (bf16[16,4,128]{2,1,0:T(4,128)(2,1)S(1)}, bf16[16,4,128]{2,1,0:T(4,128)(2,1)S(1)}, u32[]{:S(2)}, u32[]{:S(2)}) collective-permute-start(bf16[16,4,128]{2,1,0:T(4,128)(2,1)S(1)} %get-tuple-element.28), channel_id=1, source_target_pairs={{0,1},{1,2},{2,3},{3,4},{4,5},{5,6},{6,7},{8,9},{9,10},{10,11},{11... | collective-permute-start | bytes 49160 | tf_op jit(solution)/shard_map/ppermute | solution.py:17
  46.8 1.3 collective-permute-start.1
  48.1 27.1 %all-gather.3.cloned.1.call-done = bf16[2048,1152]{1,0:T(8,128)(2,1)} async-done(((bf16[512,1152]{1,0:T(8,128)(2,1)}), bf16[2048,1152]{1,0:T(8,128)(2,1)}) %all-gather.3.cloned.1.call-update) | async-done | bytes 4718608 | tf_op jit(solution)/shard_map/all_gather | solution.py:152
  75.2 1.7 fusion.92
  76.9 1.7 fusion.44
  78.6 1.5 fusion.49
  80.1 1.5 fusion.69
  81.6 1.5 fusion.41
  83.2 1.5 fusion.36
  84.7 1.5 fusion.64
  86.2 1.6 fusion.13
  87.8 2.8 %fusion.18 = bf16[16,128,128]{2,1,0:T(8,128)(2,1)} fusion(f32[128,16,128]{2,1,0:T(8,128)S(1)} %bitcast.111, f32[16,128,128]{2,1,0:T(8,128)S(1)} %fusion.64, f32[16,128,128]{2,1,0:T(8,128)S(1)} %fusion.36, f32[16,128,128]{2,1,0:T(8,128)S(1)} %fusion.41, f32[16,128,128]{2,1,0:T(8,128)S(1)} %fusion.13, bf16[16,4,128]{2,1,0:T(4,128)(2,1)S(1)} %collective-permute-done.1, ...), kind=kOutput, calls=%fused_computation.37 | convolution fusion | flops 71565312 | bytes 6832128 | tf_op jit(solution)/shard_map/gtc,goc->gto/dot_general | solution.py:42
  90.6 4.6 %all-to-all-start.3 = ((bf16[16,128,128]{2,1,0:T(8,128)(2,1)}), bf16[16,128,128]{2,1,0:T(8,128)(2,1)S(1)}, u32[]{:S(2)}, u32[]{:S(2)}) async-start(bf16[16,128,128]{2,1,0:T(8,128)(2,1)} %fusion.18), calls=%async_computation.3 | async-start | bytes 1048576 | tf_op jit(solution)/shard_map/all_to_all | solution.py:164
  95.3 0.3 copy.133
  95.6 0.2 all_to_all.49
  95.8 14.8 %all-to-all-done.3 = bf16[16,128,128]{2,1,0:T(8,128)(2,1)S(1)} async-done(((bf16[16,128,128]{2,1,0:T(8,128)(2,1)}), bf16[16,128,128]{2,1,0:T(8,128)(2,1)S(1)}, u32[]{:S(2)}, u32[]{:S(2)}) %all-to-all-start.3) | async-done | bytes 524320 | tf_op jit(solution)/shard_map/all_to_all | solution.py:164
  110.7 0.4 convolution_dynamic-update-slice_fusion.8
  111.0 0.4 convolution_dynamic-update-slice_fusion.7
  111.4 0.4 convolution_dynamic-update-slice_fusion.6
  111.7 0.4 convolution_dynamic-update-slice_fusion.5
  112.1 0.3 convolution_dynamic-update-slice_fusion.4
  112.4 0.4 convolution_dynamic-update-slice_fusion.3
  112.8 0.4 convolution_dynamic-update-slice_fusion.2
  113.1 0.4 convolution_dynamic-update-slice_fusion.1
  113.5 0.4 convolution_dynamic-update-slice_fusion
  114.0 1.4 copy.134
  115.5 0.1 copy.125
  115.6 0.8 fusion.147
  116.4 1.6 collective-permute-start.2
  118.0 1.7 fusion.90
  119.7 3.3 %collective-permute-start.3 = (bf16[16,4,128]{2,1,0:T(4,128)(2,1)S(1)}, bf16[16,4,128]{2,1,0:T(4,128)(2,1)S(1)}, u32[]{:S(2)}, u32[]{:S(2)}) collective-permute-start(bf16[16,4,128]{2,1,0:T(4,128)(2,1)S(1)} %get-tuple-element.27), channel_id=1, source_target_pairs={{0,1},{1,2},{2,3},{3,4},{4,5},{5,6},{6,7},{8,9},{9,10},{10,11},{11... | collective-permute-start | bytes 49160 | tf_op jit(solution)/shard_map/ppermute | solution.py:17
  123.0 1.7 fusion.33
  124.7 1.7 fusion.28
  126.5 1.7 fusion.59
  128.2 1.6 fusion.25
  129.8 1.6 fusion.20
  131.3 1.6 fusion.54
  132.9 1.6 fusion.7
  134.5 1.6 fusion.4
  136.0 0.3 copy.144
  136.4 0.3 multiply_reduce_fusion
  136.7 1.4 fusion.16
  138.1 0.3 copy.124
  138.5 1.3 pad_maximum_fusion
  139.8 2.8 %all-to-all-start.1 = ((bf16[32,130,64]{1,2,0:T(8,128)(2,1)}), bf16[32,130,64]{1,2,0:T(8,128)(2,1)S(1)}, u32[]{:S(2)}, u32[]{:S(2)}) async-start(bf16[32,130,64]{1,2,0:T(8,128)(2,1)} %pad_maximum_fusion), calls=%async_computation.1 | async-start | bytes 2097152 | tf_op jit(solution)/shard_map/all_to_all | solution.py:111
  142.7 27.5 %all-to-all-done.1 = bf16[32,130,64]{1,2,0:T(8,128)(2,1)S(1)} async-done(((bf16[32,130,64]{1,2,0:T(8,128)(2,1)}), bf16[32,130,64]{1,2,0:T(8,128)(2,1)S(1)}, u32[]{:S(2)}, u32[]{:S(2)}) %all-to-all-start.1) | async-done | bytes 532512 | tf_op jit(solution)/shard_map/all_to_all | solution.py:111
  170.3 0.3 copy.145
  170.8 0.9 fusion.14
  171.8 0.1 reshape.135
  171.9 9.7 %all_to_all.55 = f32[32,1,576]{2,1,0:T(1,128)S(1)} all-to-all(f32[32,1,576]{2,1,0:T(1,128)S(1)} %reshape.135), channel_id=1, replica_groups=mesh['fsdp'=4,'seq'=8] {'fsdp','seq'}, dimensions={0} | all-to-all | bytes 147456 | tf_op jit(solution)/shard_map/all_to_all | solution.py:125
  181.6 0.5 broadcast.70
  182.1 0.8 reduce.7
  183.1 0.7 reshape.123
  183.8 0.6 slice_reduce_fusion
  184.4 3.7 %reduce_sum.49 = f32[256,1152]{1,0:T(8,128)} reduce(f32[4,256,1152]{2,1,0:T(8,128)} %all-gather.5.cloned.1.call-done, f32[]{:T(128)} %constant.44.clone.1), dimensions={0}, to_apply=%region_4.5 | reduce | flops 884736 | bytes 5898244 | tf_op jit(solution)/shard_map/reduce_sum | solution.py:190
  (43 shorter events, 1.1 us)
Async XLA Ops:
  7.2 8.1 %copy-start.1 = (bf16[1,128,2048]{2,1,0:T(8,128)(2,1)S(1)}, bf16[1,128,2048]{2,1,0:T(8,128)(2,1)}, u32[]{:S(2)}) copy-start(bf16[1,128,2048]{2,1,0:T(8,128)(2,1)} %param.15) | copy-start | bytes 1572868
  7.2 28.7 %copy-start.4 = (s32[1,128]{1,0:T(1,128)S(1)}, s32[1,128]{1,0:T(1,128)}, u32[]{:S(2)}) copy-start(s32[1,128]{1,0:T(1,128)} %param.11) | copy-start | bytes 1540
  7.2 68.0 %all-gather.3.cloned.1.call-start = ((), (), s32[]{:S(2)}) async-start(), calls=%async_computation.5 | async-start | bytes 5898240 | tf_op jit(solution)/shard_map/all_gather | solution.py:152
  10.0 27.4 %copy-start.3 = (f32[2048]{0:T(1024)S(1)}, f32[2048]{0:T(1024)}, u32[]{:S(2)}) copy-start(f32[2048]{0:T(1024)} %param.13) | copy-start | bytes 24580
  10.0 25.9 %all-to-all-start = ((bf16[4,64,2048]{2,1,0:T(8,128)(2,1)}), bf16[4,64,2048]{2,1,0:T(8,128)(2,1)S(1)}, u32[]{:S(2)}, u32[]{:S(2)}) async-start(bf16[4,64,2048]{2,1,0:T(8,128)(2,1)} %tile.2), calls=%async_computation | async-start | bytes 2097152 | tf_op jit(solution)/shard_map/all_to_all | solution.py:33
  38.4 52.3 %all-to-all-start.4 = ((bf16[16,128,128]{2,1,0:T(8,128)(2,1)}), bf16[16,128,128]{2,1,0:T(8,128)(2,1)S(1)}, u32[]{:S(2)}, u32[]{:S(2)}) async-start(bf16[16,128,128]{2,1,0:T(8,128)(2,1)} %bitcast_bitcast_fusion), calls=%async_computation.4 | async-start | bytes 1048576 | tf_op jit(solution)/shard_map/all_to_all | solution.py:163
  44.4 32.5 %collective-permute-start = (bf16[16,4,128]{2,1,0:T(4,128)(2,1)S(1)}, bf16[16,4,128]{2,1,0:T(4,128)(2,1)S(1)}, u32[]{:S(2)}, u32[]{:S(2)}) collective-permute-start(bf16[16,4,128]{2,1,0:T(4,128)(2,1)S(1)} %get-tuple-element.28), channel_id=1, source_target_pairs={{0,1},{1,2},{2,3},{3,4},{4,5},{5,6},{6,7},{8,9},{9,10},{10,11},{11... | collective-permute-start | bytes 49160 | tf_op jit(solution)/shard_map/ppermute | solution.py:17
  46.8 34.8 %collective-permute-start.1 = (bf16[16,4,128]{2,1,0:T(4,128)(2,1)S(1)}, bf16[16,4,128]{2,1,0:T(4,128)(2,1)S(1)}, u32[]{:S(2)}, u32[]{:S(2)}) collective-permute-start(bf16[16,4,128]{2,1,0:T(4,128)(2,1)S(1)} %get-tuple-element.29), channel_id=1, source_target_pairs={{1,0},{2,1},{3,2},{4,3},{5,4},{6,5},{7,6},{9,8},{10,9},{11,10},{12... | collective-permute-start | bytes 49160 | tf_op jit(solution)/shard_map/ppermute | solution.py:19
  75.1 3.4 %copy-start = (bf16[2048,1152]{1,0:T(8,128)(2,1)S(1)}, bf16[2048,1152]{1,0:T(8,128)(2,1)}, u32[]{:S(2)}) copy-start(bf16[2048,1152]{1,0:T(8,128)(2,1)} %all-gather.3.cloned.1.call-done) | copy-start | bytes 14155780
  90.6 20.0 %all-to-all-start.3 = ((bf16[16,128,128]{2,1,0:T(8,128)(2,1)}), bf16[16,128,128]{2,1,0:T(8,128)(2,1)S(1)}, u32[]{:S(2)}, u32[]{:S(2)}) async-start(bf16[16,128,128]{2,1,0:T(8,128)(2,1)} %fusion.18), calls=%async_computation.3 | async-start | bytes 1048576 | tf_op jit(solution)/shard_map/all_to_all | solution.py:164
  95.2 89.1 %all-gather.5.cloned.1.call-start = ((), (), s32[]{:S(2)}) async-start(), calls=%async_computation.6 | async-start | bytes 5898240 | tf_op jit(solution)/shard_map/all_gather | solution.py:189
  113.9 14.3 %slice-start = ((s8[4718592]{0:T(1024)(128)(4,1)}), s8[524288]{0:T(1024)(128)(4,1)S(1)}, s32[]{:S(2)}) async-start(s8[4718592]{0:T(1024)(128)(4,1)} %bitcast.88), calls=%async_computation.7 | async-start | bytes 1048576
  116.4 11.8 %slice-start.1 = ((s8[4718592]{0:T(1024)(128)(4,1)}), s8[4194304]{0:T(1024)(128)(4,1)S(1)}, s32[]{:S(2)}) async-start(s8[4718592]{0:T(1024)(128)(4,1)} %bitcast.88), calls=%async_computation.8 | async-start | bytes 8388608
  116.4 6.6 %collective-permute-start.2 = (bf16[16,4,128]{2,1,0:T(4,128)(2,1)S(1)}, bf16[16,4,128]{2,1,0:T(4,128)(2,1)S(1)}, u32[]{:S(2)}, u32[]{:S(2)}) collective-permute-start(bf16[16,4,128]{2,1,0:T(4,128)(2,1)S(1)} %get-tuple-element.26), channel_id=1, source_target_pairs={{1,0},{2,1},{3,2},{4,3},{5,4},{6,5},{7,6},{9,8},{10,9},{11,10},{12... | collective-permute-start | bytes 49160 | tf_op jit(solution)/shard_map/ppermute | solution.py:19
  119.7 8.5 %collective-permute-start.3 = (bf16[16,4,128]{2,1,0:T(4,128)(2,1)S(1)}, bf16[16,4,128]{2,1,0:T(4,128)(2,1)S(1)}, u32[]{:S(2)}, u32[]{:S(2)}) collective-permute-start(bf16[16,4,128]{2,1,0:T(4,128)(2,1)S(1)} %get-tuple-element.27), channel_id=1, source_target_pairs={{0,1},{1,2},{2,3},{3,4},{4,5},{5,6},{6,7},{8,9},{9,10},{10,11},{11... | collective-permute-start | bytes 49160 | tf_op jit(solution)/shard_map/ppermute | solution.py:17
  138.1 33.5 %copy-start.2 = (bf16[128,2048]{1,0:T(8,128)(2,1)}, bf16[128,2048]{1,0:T(8,128)(2,1)S(1)}, u32[]{:S(2)}) copy-start(bf16[128,2048]{1,0:T(8,128)(2,1)S(1)} %fusion.16) | copy-start | bytes 1572868
  139.8 30.4 %all-to-all-start.1 = ((bf16[32,130,64]{1,2,0:T(8,128)(2,1)}), bf16[32,130,64]{1,2,0:T(8,128)(2,1)S(1)}, u32[]{:S(2)}, u32[]{:S(2)}) async-start(bf16[32,130,64]{1,2,0:T(8,128)(2,1)} %pad_maximum_fusion), calls=%async_computation.1 | async-start | bytes 2097152 | tf_op jit(solution)/shard_map/all_to_all | solution.py:111
Sparse Core Ops, SparseCore 0:
  9.9 65.2 all-gather.2
  115.5 67.0 all-gather.4
